TPU v7x, 128 devices: a whole 4x4x4 slice. The times are simulated.
128 devices in a mesh: section: 2 (over z_lo), cp: 16 (over y, z_hi, core), tp: 4 (over x).
Axes of the slice: x: 4, y: 4, z: 4 (z_hi: 2, z_lo: 2; z = z_hi * 2 + z_lo), core: 2. Of those that a mesh axis runs over, the one named last changes fastest.
Arguments:
- rollout_rows: bfloat16 [2048, 8192], P(('section', 'cp'), 'tp'), may hold values from -60 to 60
- lengths: int32 [2], replicated, may hold values from 1 to 1536, 2048 in all
- block_owner: int32 [32], replicated, may hold values from 0 to 31, each once
- norm_gain: float32 [2, 8192], P('section', 'tp'), may hold values from 0.1 to 1.9
- w_qkv: bfloat16 [2, 3, 8192, 8192], P('section', None, 'tp', 'cp'), may hold values from -1 to 1
- w_out: bfloat16 [2, 8192, 8192], P('section', 'cp', 'tp'), may hold values from -0.5 to 0.5
Outputs:
- scored: bfloat16 [2, 2048, 8192], P(None, ('section', 'cp'), 'tp')
Inputs may be any that keep to these rules, and one draw needn't show every extreme that they name: The 2 lengths sum to 2048; neither is over 1536. `block_owner`: every owner block appears once.
All inputs are finite; a program needn't handle non-finite values.
Results may differ from a plain program's by a relative error of at most 0.022.
Values may be sent and summed in bfloat16 or wider, within the bound.
No kernel may reach another device: no remote copies, remote signals or barrier semaphores. Data moves between devices by JAX's collectives and lax.ppermute only.
A program may use at most 128 MiB of HBM per device.

v0:
```python
import math
import jax
import jax.numpy as jnp
from jax import lax
from jax.sharding import PartitionSpec as P

D = 8192
HEAD = 128


def layout_position(layout_rows, tokens, tp_count):
    quarter = tokens // tp_count
    halfblock = quarter // 2
    owner_index = layout_rows // quarter
    second = layout_rows % quarter // halfblock
    offset = layout_rows % halfblock
    block_index = 2 * owner_index + second
    return block_index * halfblock + offset


def layout_row(position, tokens, tp_count):
    quarter = tokens // tp_count
    halfblock = quarter // 2
    block_index = position // halfblock
    offset = position % halfblock
    second = block_index % 2
    owner_index = block_index // 2
    return owner_index * quarter + second * halfblock + offset


def on_device(rollout_rows, lengths, block_owner, norm_gain, w_qkv, w_out):
    tp_count = lax.axis_size("tp")
    cp_count = lax.axis_size("cp")
    sections = lax.axis_size("section")
    own_rows, width_here = rollout_rows.shape
    blocks = sections * cp_count
    tokens = own_rows * blocks
    actor_rows = lax.all_gather(rollout_rows, ("section", "cp"), axis=0, tiled=True)
    layout_rows = jnp.arange(tokens, dtype=jnp.int32)
    position = layout_position(layout_rows, tokens, tp_count)
    source = block_owner[position // own_rows] * own_rows + position % own_rows
    rows_in = jnp.take(actor_rows, source, axis=0)
    seq_ends = jnp.cumsum(lengths)
    sequence = jnp.sum((position[:, None] >= seq_ends[None, :]).astype(jnp.int32), axis=1)
    squares = jnp.sum(jnp.square(rows_in.astype(jnp.float32)), axis=1)
    total_squares = lax.psum(squares, "tp")
    inverse_rms = lax.rsqrt(total_squares / D + 1e-05)
    normed = (rows_in.astype(jnp.float32) * norm_gain[0][None, :] * inverse_rms[:, None]).astype(
        jnp.bfloat16
    )
    qkv_weights = w_qkv[0]
    local_rows = tokens // tp_count
    halfblock = local_rows // 2
    heads_here = qkv_weights.shape[2] // HEAD
    first_local = lax.axis_index("tp") * local_rows
    query_pos = lax.dynamic_slice_in_dim(position, first_local, local_rows, 0).reshape(2, halfblock)
    query_seq = lax.dynamic_slice_in_dim(sequence, first_local, local_rows, 0).reshape(2, halfblock)
    inv_sqrt = 1.0 / math.sqrt(HEAD)
    initial = (
        jnp.full((2, heads_here, halfblock), -1e30, jnp.float32),
        jnp.zeros((2, heads_here, halfblock), jnp.float32),
        jnp.zeros((2, heads_here, halfblock, HEAD), jnp.float32),
    )
    projected = lax.psum_scatter(
        jnp.einsum("rd,kdc->rkc", normed, qkv_weights, preferred_element_type=jnp.float32),
        "tp",
        scatter_dimension=0,
        tiled=True,
    ).astype(jnp.bfloat16)
    query_blocks = projected[:, 0].reshape(2, halfblock, heads_here, HEAD)
    key_part = lax.all_gather(projected[:, 1], "tp", axis=0, tiled=True)
    value_part = lax.all_gather(projected[:, 2], "tp", axis=0, tiled=True)
    key_count = key_part.shape[0]
    key_heads = key_part.reshape(key_count, heads_here, HEAD)
    value_heads = value_part.reshape(key_count, heads_here, HEAD)
    results = []
    for sub_block in range(2):
        allowed = (query_seq[sub_block][:, None] == sequence[None, :]) & (
            position[None, :] <= query_pos[sub_block][:, None]
        )
        query_block = query_blocks[sub_block]

        def update(state_now):
            row_peak, row_total, weighted = state_now
            scores = (
                jnp.einsum(
                    "qhd,khd->hqk", query_block, key_heads, preferred_element_type=jnp.float32
                )
                * inv_sqrt
            )
            scores = jnp.where(allowed[None], scores, -1e30)
            new_peak = jnp.maximum(row_peak, jnp.max(scores, axis=2))
            weights_now = jnp.where(allowed[None], jnp.exp(scores - new_peak[:, :, None]), 0.0)
            row_total = jnp.sum(weights_now, axis=2)
            probabilities = weights_now.astype(jnp.bfloat16)
            weighted = jnp.einsum(
                "hqk,khd->hqd", probabilities, value_heads, preferred_element_type=jnp.float32
            )
            return (new_peak, row_total, weighted)

        def unchanged(state_now):
            return state_now

        results.append(
            lax.cond(
                jnp.any(allowed),
                update,
                unchanged,
                (initial[0][sub_block], initial[1][sub_block], initial[2][sub_block]),
            )
        )
    attended = (
        jnp.stack([results[0][2], results[1][2]])
        / jnp.stack([results[0][1], results[1][1]])[:, :, :, None]
    )
    attended = (
        attended.transpose(0, 2, 1, 3).reshape(local_rows, heads_here * HEAD).astype(jnp.bfloat16)
    )
    gathered = lax.all_gather(attended, "tp", axis=0, tiled=True)
    group_rows = sections * own_rows
    target_rows = jnp.arange(tokens, dtype=jnp.int32)
    cp_index = target_rows // group_rows
    owner_section = target_rows % group_rows // own_rows
    inner = target_rows % own_rows
    actor_block = owner_section * cp_count + cp_index
    block_ids = jnp.arange(blocks, dtype=jnp.int32)
    inverse_owner = jnp.sum(
        jnp.where(block_owner[None, :] == block_ids[:, None], block_ids[None, :], 0), axis=1
    )
    packed_pos = inverse_owner[actor_block] * own_rows + inner
    ordered = jnp.take(gathered, layout_row(packed_pos, tokens, tp_count), axis=0)
    out_weight = w_out[0]
    summed = lax.psum_scatter(
        jnp.dot(ordered, out_weight, preferred_element_type=jnp.float32).astype(jnp.bfloat16),
        "cp",
        scatter_dimension=0,
        tiled=True,
    )
    branch = summed.reshape(sections, own_rows, width_here)
    return lax.all_to_all(branch, "section", split_axis=0, concat_axis=0, tiled=True)


def solution(mesh):
    return jax.shard_map(
        on_device,
        mesh=mesh,
        in_specs=(
            P(("section", "cp"), "tp"),
            P(),
            P(),
            P("section", "tp"),
            P("section", None, "tp", "cp"),
            P("section", "cp", "tp"),
        ),
        out_specs=P(None, ("section", "cp"), "tp"),
        check_vma=False,
    )
```

profile of v0, /device:TPU:0, one launch (start us, length us, event | category | flops | bytes accessed | tf_op | source)
XLA Modules:
  0.0 519.2 jit_solution(15395411485198232677)
XLA Ops:
  14.3 4.6 compare_select_fusion.4
  18.9 15.4 %compare_and_fusion.2 = (pred[2048]{0:T(1024)(128)(4,1)S(1)}, s32[2048]{0:T(1024)S(1)}) fusion(pred[2048]{0:T(1024)(128)(4,1)S(1)} %compare_reduce_fusion, pred[2048]{0:T(1024)(128)(4,1)S(1)} %compare_reduce_fusion.1, pred[2048]{0:T(1024)(128)(4,1)S(1)} %compare_reduce_fusion.2, pred[2048]{0:T(1024)(128)(4,1)S(1)} %compare_reduce_fusion.3, ...), kind=kLoop, calls=%fused_computation.236 | loop fusion | flops 165888 | bytes 69732 | tf_op jit(solution)/shard_map/jit(_take)/and | solution.py:42
  34.4 43.7 %all-gather.7.cloned.1.call-done = bf16[2048,2048]{1,0:T(8,128)(2,1)} async-done(((bf16[64,2048]{1,0:T(8,128)(2,1)}), bf16[2048,2048]{1,0:T(8,128)(2,1)}) %all-gather.7.cloned.1.call-update) | async-done | bytes 8388624 | tf_op jit(solution)/shard_map/all_gather | solution.py:38
  78.0 20.8 %gather_fusion = bf16[2048,2048]{1,0:T(8,128)(2,1)} fusion(bf16[2048,2048]{1,0:T(8,128)(2,1)} %all-gather.7.cloned.1.call-done, s32[2048]{0:T(1024)S(1)} %broadcast_clamp_fusion.1), kind=kCustom, calls=%fused_computation | custom fusion | bytes 16785408 | tf_op jit(solution)/shard_map/jit(_take)/gather | solution.py:42
  98.8 5.7 %fusion.36 = f32[2048]{0:T(1024)S(1)} fusion(bf16[2048,2048]{1,0:T(8,128)(2,1)} %gather_fusion, pred[2048]{0:T(1024)(128)(4,1)S(1)} %get-tuple-element.73), kind=kLoop, calls=%fused_computation.36 | loop fusion | flops 16775168 | bytes 8398848 | tf_op jit(solution)/shard_map/reduce_sum | solution.py:45
  104.6 10.7 %psum.7 = f32[2048]{0:T(1024)S(1)} all-reduce(f32[2048]{0:T(1024)S(1)} %fusion.36), channel_id=1, replica_groups=mesh['section'=2,'cp'=16,'tp'=4] {'tp'}, use_global_device_ids=true, to_apply=%region_5.6 | all-reduce | flops 2048 | bytes 16384 | tf_op jit(solution)/shard_map/psum | solution.py:46
  115.3 20.0 %fusion.38 = f32[2048,3,512]{2,0,1:T(8,128)} fusion(f32[2048]{0:T(1024)S(1)} %add_rsqrt_fusion, f32[2048]{0:T(1024)S(1)} %bitcast.118, bf16[1,3,2048,512]{3,2,1,0:T(8,128)(2,1)} %param.14, bf16[2048,2048]{1,0:T(8,128)(2,1)} %gather_fusion, pred[2048]{0:T(1024)(128)(4,1)S(1)} %get-tuple-element.73), kind=kOutput, calls=%fused_computation.38 | convolution fusion | flops 12905873408 | bytes 27281408 | tf_op jit(solution)/shard_map/rd,kdc->rkc/dot_general | solution.py:65
  135.4 111.7 %reduce-scatter.3.cloned.1.call-done = f32[512,3,512]{2,0,1:T(8,128)} async-done(((f32[2048,3,512]{2,0,1:T(8,128)}), f32[512,3,512]{2,0,1:T(8,128)}) %reduce-scatter.3.cloned.1.call-update) | async-done | bytes 3145744 | tf_op jit(solution)/shard_map/reduce_scatter | solution.py:64
  255.7 26.5 %all-gather.11.cloned.1.call-done = bf16[2048,1,512]{2,0,1:T(8,128)(2,1)} async-done(((bf16[512,1,512]{2,0,1:T(8,128)(2,1)}), bf16[2048,1,512]{2,0,1:T(8,128)(2,1)}) %all-gather.11.cloned.1.call-update) | async-done | bytes 2097168 | tf_op jit(solution)/shard_map/all_gather | solution.py:71
  282.2 4.0 reshape.639
  286.2 28.4 %all-gather.13.cloned.1.call-done = bf16[2048,1,512]{2,0,1:T(8,128)(2,1)} async-done(((bf16[512,1,512]{2,0,1:T(8,128)(2,1)}), bf16[2048,1,512]{2,0,1:T(8,128)(2,1)}) %all-gather.13.cloned.1.call-update) | async-done | bytes 2097168 | tf_op jit(solution)/shard_map/all_gather | solution.py:72
  314.6 4.0 reshape.640
  318.6 13.3 %conditional.2 = (f32[1,4,256]{2,1,0:T(4,128)S(1)}, f32[1,4,256,128]{3,2,1,0:T(8,128)}) conditional(s32[]{:T(128)} %convert_element_type.38, () %tuple.29, (pred[256,2048]{1,0:T(8,128)(4,1)S(1)}, bf16[512,3,512]{2,0,1:T(8,128)(2,1)}, bf16[2048,4,128]{2,1,0:T(4,128)(2,1)}, bf16[2048,4,128]{2,1,0:T(4,128)(2,1)}) %tuple.128), branch_computations={%region_7.8_spmd, %region_8.11_spmd} | conditional | flops 1101003776 | bytes 43802668 | solution.py:105
  322.3 3.7 fusion
  326.0 3.4 fusion.9
  331.9 12.8 %conditional.3 = (f32[1,4,256]{2,1,0:T(4,128)S(1)}, f32[1,4,256,128]{3,2,1,0:T(8,128)S(1)}) conditional(s32[]{:T(128)} %convert_element_type.42, () %tuple.31, (pred[256,2048]{1,0:T(8,128)(4,1)S(1)}, bf16[512,3,512]{2,0,1:T(8,128)(2,1)}, bf16[2048,4,128]{2,1,0:T(4,128)(2,1)}, bf16[2048,4,128]{2,1,0:T(4,128)(2,1)}) %tuple.129), branch_computations={%region_12.13_spmd, %region_13.16_spmd} | conditional | flops 1101003776 | bytes 43802668 | solution.py:105
  335.9 3.7 fusion.17
  351.7 4.6 compare_select_fusion.10
  356.3 15.4 %compare_and_fusion.3 = (pred[2048]{0:T(1024)(128)(4,1)S(1)}, s32[2048]{0:T(1024)S(1)}) fusion(pred[2048]{0:T(1024)(128)(4,1)S(1)} %compare_reduce_fusion.25, pred[2048]{0:T(1024)(128)(4,1)S(1)} %compare_reduce_fusion.26, pred[2048]{0:T(1024)(128)(4,1)S(1)} %compare_reduce_fusion.27, pred[2048]{0:T(1024)(128)(4,1)S(1)} %compare_reduce_fusion.28, ...), kind=kLoop, calls=%fused_computation.237 | loop fusion | flops 165888 | bytes 69732 | tf_op jit(solution)/shard_map/jit(_take)/and | solution.py:131
  371.9 6.6 %all-gather.9.cloned.1.call-done = bf16[2048,512]{1,0:T(8,128)(2,1)} async-done(((bf16[512,512]{1,0:T(8,128)(2,1)}), bf16[2048,512]{1,0:T(8,128)(2,1)}) %all-gather.9.cloned.1.call-update) | async-done | bytes 2097168 | tf_op jit(solution)/shard_map/all_gather | solution.py:119
  378.5 11.1 %gather_fusion.1 = bf16[2048,512]{1,0:T(8,128)(2,1)} fusion(bf16[2048,512]{1,0:T(8,128)(2,1)} %all-gather.9.cloned.1.call-done, s32[2048]{0:T(1024)S(1)} %broadcast_clamp_fusion), kind=kCustom, calls=%fused_computation.1 | custom fusion | bytes 4202496 | tf_op jit(solution)/shard_map/jit(_take)/gather | solution.py:131
  389.5 8.5 %convolution_convert_fusion = bf16[2048,2048]{1,0:T(8,128)(2,1)} fusion(bf16[1,512,2048]{2,1,0:T(8,128)(2,1)S(1)} %copy-done, bf16[2048,512]{1,0:T(8,128)(2,1)} %gather_fusion.1, pred[2048]{0:T(1024)(128)(4,1)S(1)} %get-tuple-element.69), kind=kOutput, calls=%fused_computation.42 | convolution fusion | flops 4300210176 | bytes 12584960 | tf_op jit(solution)/shard_map/dot_general | solution.py:134
  398.0 102.8 %reduce-scatter.5.cloned.1.call-done = bf16[128,2048]{1,0:T(8,128)(2,1)} async-done(((bf16[2048,2048]{1,0:T(8,128)(2,1)}), bf16[128,2048]{1,0:T(8,128)(2,1)}) %reduce-scatter.5.cloned.1.call-update) | async-done | bytes 524304 | tf_op jit(solution)/shard_map/reduce_scatter | solution.py:133
  500.8 10.7 %all_to_all.5 = bf16[2,64,2048]{2,1,0:T(8,128)(2,1)S(1)} all-to-all(bf16[2,64,2048]{2,1,0:T(8,128)(2,1)} %bitcast.108), channel_id=1, replica_groups=mesh['section'=2,'cp'=16,'tp'=4] {'section'}, dimensions={0} | all-to-all | bytes 1048576 | tf_op jit(solution)/shard_map/all_to_all | solution.py:140
  (109 shorter events, 38.0 us)
Async XLA Ops:
  6.5 383.0 %copy-start = (bf16[1,512,2048]{2,1,0:T(8,128)(2,1)S(1)}, bf16[1,512,2048]{2,1,0:T(8,128)(2,1)}, u32[]{:S(2)}) copy-start(bf16[1,512,2048]{2,1,0:T(8,128)(2,1)} %param.15) | copy-start | bytes 6291460
  6.5 71.5 %all-gather.7.cloned.1.call-start = ((), (), s32[]{:S(2)}) async-start(), calls=%async_computation.3 | async-start | bytes 8650752 | tf_op jit(solution)/shard_map/all_gather | solution.py:38
  7.3 239.9 %reduce-scatter.3.cloned.1.call-start = ((), (), s32[]{:S(2)}) async-start(), calls=%async_computation.4 | async-start | bytes 15728640 | tf_op jit(solution)/shard_map/reduce_scatter | solution.py:64
  98.8 16.5 %copy-start.5 = (f32[1,2048]{1,0:T(1,128)S(1)}, f32[1,2048]{1,0:T(1,128)}, u32[]{:S(2)}) copy-start(f32[1,2048]{1,0:T(1,128)} %param.13) | copy-start | bytes 24580
  135.4 116.9 %copy-start.6 = (s32[2]{0:T(128)S(1)}, s32[2]{0:T(128)}, u32[]{:S(2)}) copy-start(s32[2]{0:T(128)} %param.11) | copy-start | bytes 28
  135.4 146.8 %all-gather.11.cloned.1.call-start = ((), (), s32[]{:S(2)}) async-start(), calls=%async_computation.7 | async-start | bytes 2621440 | tf_op jit(solution)/shard_map/all_gather | solution.py:71
  249.3 1.1 copy-start.1
  251.5 63.1 %all-gather.13.cloned.1.call-start = ((), (), s32[]{:S(2)}) async-start(), calls=%async_computation.8 | async-start | bytes 2621440 | tf_op jit(solution)/shard_map/all_gather | solution.py:72
  252.1 126.4 %all-gather.9.cloned.1.call-start = ((), (), s32[]{:S(2)}) async-start(), calls=%async_computation.5 | async-start | bytes 2621440 | tf_op jit(solution)/shard_map/all_gather | solution.py:119
  321.1 4.8 copy-start.2
  331.9 18.2 %copy-start.4 = (s32[32]{0:T(128)S(1)}, s32[32]{0:T(128)}, u32[]{:S(2)}) copy-start(s32[32]{0:T(128)} %param.12) | copy-start | bytes 388
  334.8 4.8 copy-start.3
  347.5 153.4 %reduce-scatter.5.cloned.1.call-start = ((), (), s32[]{:S(2)}) async-start(), calls=%async_computation.6 | async-start | bytes 8912896 | tf_op jit(solution)/shard_map/reduce_scatter | solution.py:133
Sparse Core Ops, SparseCore 0:
  9.1 68.9 all-gather.6
  135.5 111.6 reduce-scatter.2
  251.6 30.5 all-gather.10
  283.7 30.8 all-gather.12
  347.6 30.8 all-gather.8
  398.1 102.6 reduce-scatter.4
where the time goes:
time: 521 us; the launch traced here: 519 us
  waiting for transfers between devices  321 us (62%)
  other arithmetic  62.2 us (12%)
  local copies, waits for them, and re-layouts  57 us (11%)
  matrix products  42 us (8%)
  blocking collectives  21.5 us (4%)
  between operations  14.9 us (3%)
    reduce_scatter x1, waiting for transfers between devices, on_device(): lax.psum_scatter(jnp.einsum('rd,kdc->rkc', normed, qkv_weights, preferred...  112 us
    reduce_scatter x1, waiting for transfers between devices, on_device(): lax.psum_scatter(jnp.dot(ordered, out_weight, preferred_element_type=jnp....  103 us
    all_gather x1, waiting for transfers between devices, on_device(): lax.all_gather(rollout_rows, ('section', 'cp'), axis=0, tiled=True)  43.7 us
    all_gather x1, waiting for transfers between devices, on_device(): value_part = lax.all_gather(projected[:, 2], 'tp', axis=0, tiled=True)  28.4 us
    all_gather x1, waiting for transfers between devices, on_device(): key_part = lax.all_gather(projected[:, 1], 'tp', axis=0, tiled=True)  26.5 us
    gather x1, local copies, waits for them, and re-layouts, on_device(): rows_in = jnp.take(actor_rows, source, axis=0)  20.8 us
    dot_general x1, matrix products, on_device(): jnp.einsum('rd,kdc->rkc', normed, qkv_weights, preferred_element_type=jnp...  20 us
    and x1, other arithmetic, on_device(): jnp.take(gathered, layout_row(packed_pos, tokens, tp_count), axis=0)  15.4 us
  transfers between devices with their start and end apart: 6, of which 6 were waited for; matrix products, arithmetic and copies ran while one was open for 11% of the time, Pallas kernels for 0%

commit v1 on v0

--- a/solution.py
+++ b/solution.py
@@ -6,6 +6,19 @@
 
 D = 8192
 HEAD = 128
+
+
+def gather_around(x, axis, dim):
+    ways = lax.axis_size(axis)
+    up = [(d, (d + 1) % ways) for d in range(ways)]
+    down = [(d, (d - 1) % ways) for d in range(ways)]
+    earlier, later = ([x], [x])
+    for _ in range(ways // 2):
+        earlier.append(lax.ppermute(earlier[-1], axis, up))
+    for _ in range((ways - 1) // 2):
+        later.append(lax.ppermute(later[-1], axis, down))
+    line = jnp.concatenate([*earlier[::-1], *later[1:]], axis=dim)
+    return jnp.roll(line, (lax.axis_index(axis) - ways // 2) * x.shape[dim], axis=dim)
 
 
 def layout_position(layout_rows, tokens, tp_count):
@@ -69,7 +82,7 @@
     ).astype(jnp.bfloat16)
     query_blocks = projected[:, 0].reshape(2, halfblock, heads_here, HEAD)
     key_part = lax.all_gather(projected[:, 1], "tp", axis=0, tiled=True)
-    value_part = lax.all_gather(projected[:, 2], "tp", axis=0, tiled=True)
+    value_part = gather_around(projected[:, 2], "tp", 0)
     key_count = key_part.shape[0]
     key_heads = key_part.reshape(key_count, heads_here, HEAD)
     value_heads = value_part.reshape(key_count, heads_here, HEAD)

time: 521 us -> 513 us (0.985)
  waiting for transfers between devices: 321 us -> 301 us
  local copies, waits for them, and re-layouts: 57 us -> 67.1 us
    ppermute x0 -> x3, waiting for transfers between devices: none -> 36.6 us  [the longest x2 36.6 us: gather_around(): earlier.append(lax.ppermute(earlier[-1], axis, up))]
    all_gather x1 -> x0, waiting for transfers between devices: 28.4 us -> none  [on_device(): value_part = lax.all_gather(projected[:, 2], 'tp', axis=0, tiled=True)]
    all_gather x1, waiting for transfers between devices: 26.5 us -> 0.01 us  [on_device(): key_part = lax.all_gather(projected[:, 1], 'tp', axis=0, tiled=True)]
    unnamed x12 -> x19, local copies, waits for them, and re-layouts: 2.82 us -> 10.4 us
    dynamic_slice x0 -> x2, local copies, waits for them, and re-layouts: none -> 5.44 us  [gather_around(): jnp.roll(line, (lax.axis_index(axis) - ways // 2) * x.shape[dim], axis=dim)]
  transfers between devices with their start and end apart: 6 -> 8, of which waited for: 6 -> 6; matrix products, arithmetic and copies ran while one was open for 11% -> 13% of each run, Pallas kernels for 0% -> 0%
where the time goes in v1:
time: 513 us; the launch traced here: 511 us
  waiting for transfers between devices  301 us (59%)
  local copies, waits for them, and re-layouts  67.1 us (13%)
  other arithmetic  62.1 us (12%)
  matrix products  41.1 us (8%)
  blocking collectives  21.2 us (4%)
  between operations  14.5 us (3%)
    reduce_scatter x1, waiting for transfers between devices, on_device(): lax.psum_scatter(jnp.einsum('rd,kdc->rkc', normed, qkv_weights, preferred...  112 us
    reduce_scatter x1, waiting for transfers between devices, on_device(): lax.psum_scatter(jnp.dot(ordered, out_weight, preferred_element_type=jnp....  103 us
    all_gather x1, waiting for transfers between devices, on_device(): lax.all_gather(rollout_rows, ('section', 'cp'), axis=0, tiled=True)  43.7 us
    ppermute x2, waiting for transfers between devices, gather_around(): earlier.append(lax.ppermute(earlier[-1], axis, up))  36.6 us
    gather x1, local copies, waits for them, and re-layouts, on_device(): rows_in = jnp.take(actor_rows, source, axis=0)  20.8 us
    dot_general x1, matrix products, on_device(): jnp.einsum('rd,kdc->rkc', normed, qkv_weights, preferred_element_type=jnp...  20 us
    and x1, other arithmetic, on_device(): jnp.take(gathered, layout_row(packed_pos, tokens, tp_count), axis=0)  15.4 us
    and x1, other arithmetic, on_device(): rows_in = jnp.take(actor_rows, source, axis=0)  15.4 us
  transfers between devices with their start and end apart: 8, of which 6 were waited for; matrix products, arithmetic and copies ran while one was open for 13% of the time, Pallas kernels for 0%

profile of v1, /device:TPU:0, one launch (start us, length us, event | category | flops | bytes accessed | tf_op | source)
XLA Modules:
  0.0 511.1 jit_solution(6483839448546189876)
XLA Ops:
  14.3 4.6 compare_select_fusion.4
  18.9 15.4 %compare_and_fusion.2 = (pred[2048]{0:T(1024)(128)(4,1)S(1)}, s32[2048]{0:T(1024)S(1)}) fusion(pred[2048]{0:T(1024)(128)(4,1)S(1)} %compare_reduce_fusion, pred[2048]{0:T(1024)(128)(4,1)S(1)} %compare_reduce_fusion.1, pred[2048]{0:T(1024)(128)(4,1)S(1)} %compare_reduce_fusion.2, pred[2048]{0:T(1024)(128)(4,1)S(1)} %compare_reduce_fusion.3, ...), kind=kLoop, calls=%fused_computation.243 | loop fusion | flops 165888 | bytes 69732 | tf_op jit(solution)/shard_map/jit(_take)/and | solution.py:55
  34.4 43.7 %all-gather.5.cloned.1.call-done = bf16[2048,2048]{1,0:T(8,128)(2,1)} async-done(((bf16[64,2048]{1,0:T(8,128)(2,1)}), bf16[2048,2048]{1,0:T(8,128)(2,1)}) %all-gather.5.cloned.1.call-update) | async-done | bytes 8388624 | tf_op jit(solution)/shard_map/all_gather | solution.py:51
  78.0 20.8 %gather_fusion = bf16[2048,2048]{1,0:T(8,128)(2,1)} fusion(bf16[2048,2048]{1,0:T(8,128)(2,1)} %all-gather.5.cloned.1.call-done, s32[2048]{0:T(1024)S(1)} %broadcast_clamp_fusion.1), kind=kCustom, calls=%fused_computation | custom fusion | bytes 16785408 | tf_op jit(solution)/shard_map/jit(_take)/gather | solution.py:55
  98.8 5.7 %fusion.30 = f32[2048]{0:T(1024)S(1)} fusion(bf16[2048,2048]{1,0:T(8,128)(2,1)} %gather_fusion, pred[2048]{0:T(1024)(128)(4,1)S(1)} %get-tuple-element.73), kind=kLoop, calls=%fused_computation.34 | loop fusion | flops 16775168 | bytes 8398848 | tf_op jit(solution)/shard_map/reduce_sum | solution.py:58
  104.6 10.7 %psum.7 = f32[2048]{0:T(1024)S(1)} all-reduce(f32[2048]{0:T(1024)S(1)} %fusion.30), channel_id=1, replica_groups=mesh['section'=2,'cp'=16,'tp'=4] {'tp'}, use_global_device_ids=true, to_apply=%region_5.6 | all-reduce | flops 2048 | bytes 16384 | tf_op jit(solution)/shard_map/psum | solution.py:59
  115.3 20.0 %fusion.32 = f32[2048,3,512]{2,0,1:T(8,128)} fusion(f32[2048]{0:T(1024)S(1)} %add_rsqrt_fusion, f32[2048]{0:T(1024)S(1)} %bitcast.127, bf16[1,3,2048,512]{3,2,1,0:T(8,128)(2,1)} %param.14, bf16[2048,2048]{1,0:T(8,128)(2,1)} %gather_fusion, pred[2048]{0:T(1024)(128)(4,1)S(1)} %get-tuple-element.73), kind=kOutput, calls=%fused_computation.36 | convolution fusion | flops 12905873408 | bytes 27281408 | tf_op jit(solution)/shard_map/rd,kdc->rkc/dot_general | solution.py:78
  135.5 111.7 %reduce-scatter.3.cloned.1.call-done = f32[512,3,512]{2,0,1:T(8,128)} async-done(((f32[2048,3,512]{2,0,1:T(8,128)}), f32[512,3,512]{2,0,1:T(8,128)}) %reduce-scatter.3.cloned.1.call-update) | async-done | bytes 3145744 | tf_op jit(solution)/shard_map/reduce_scatter | solution.py:77
  252.3 17.3 %collective-permute-done = bf16[512,512]{1,0:T(8,128)(2,1)} collective-permute-done((bf16[512,512]{1,0:T(8,128)(2,1)}, bf16[512,512]{1,0:T(8,128)(2,1)}, u32[]{:S(2)}, u32[]{:S(2)}) %collective-permute-start) | collective-permute-done | bytes 524320 | tf_op jit(solution)/shard_map/ppermute | solution.py:17
  269.6 3.2 collective-permute-start.2
  275.6 19.3 %collective-permute-done.1 = bf16[512,512]{1,0:T(8,128)(2,1)} collective-permute-done((bf16[512,512]{1,0:T(8,128)(2,1)}, bf16[512,512]{1,0:T(8,128)(2,1)}, u32[]{:S(2)}, u32[]{:S(2)}) %collective-permute-start.1) | collective-permute-done | bytes 524320 | tf_op jit(solution)/shard_map/ppermute | solution.py:17
  305.1 4.0 copy.24
  309.0 4.0 reshape.639
  313.0 12.9 %conditional.2 = (f32[1,4,256]{2,1,0:T(4,128)S(1)}, f32[1,4,256,128]{3,2,1,0:T(8,128)}) conditional(s32[]{:T(128)} %convert_element_type.38, () %tuple.29, (pred[256,2048]{1,0:T(8,128)(4,1)S(1)}, bf16[512,3,512]{2,0,1:T(8,128)(2,1)}, bf16[2048,4,128]{2,1,0:T(4,128)(2,1)}, bf16[2048,4,128]{0,2,1:T(8,128)(2,1)}) %tuple.128), branch_computations={%region_7.8_spmd, %region_8.11_spmd} | conditional | flops 1101003776 | bytes 43802668 | solution.py:118
  316.7 3.7 fusion
  326.0 12.4 %conditional.3 = (f32[1,4,256]{2,1,0:T(4,128)S(1)}, f32[1,4,256,128]{3,2,1,0:T(8,128)S(1)}) conditional(s32[]{:T(128)} %convert_element_type.42, () %tuple.31, (pred[256,2048]{1,0:T(8,128)(4,1)S(1)}, bf16[512,3,512]{2,0,1:T(8,128)(2,1)}, bf16[2048,4,128]{2,1,0:T(4,128)(2,1)}, bf16[2048,4,128]{0,2,1:T(8,128)(2,1)}) %tuple.129), branch_computations={%region_12.13_spmd, %region_13.16_spmd} | conditional | flops 1101003776 | bytes 43802668 | solution.py:118
  329.9 3.7 fusion.14
  345.3 4.6 compare_select_fusion.10
  349.9 15.4 %compare_and_fusion.3 = (pred[2048]{0:T(1024)(128)(4,1)S(1)}, s32[2048]{0:T(1024)S(1)}) fusion(pred[2048]{0:T(1024)(128)(4,1)S(1)} %compare_reduce_fusion.25, pred[2048]{0:T(1024)(128)(4,1)S(1)} %compare_reduce_fusion.26, pred[2048]{0:T(1024)(128)(4,1)S(1)} %compare_reduce_fusion.27, pred[2048]{0:T(1024)(128)(4,1)S(1)} %compare_reduce_fusion.28, ...), kind=kLoop, calls=%fused_computation.244 | loop fusion | flops 165888 | bytes 69732 | tf_op jit(solution)/shard_map/jit(_take)/and | solution.py:144
  365.5 5.4 %all-gather.7.cloned.1.call-done = bf16[2048,512]{1,0:T(8,128)(2,1)} async-done(((bf16[512,512]{1,0:T(8,128)(2,1)}), bf16[2048,512]{1,0:T(8,128)(2,1)}) %all-gather.7.cloned.1.call-update) | async-done | bytes 2097168 | tf_op jit(solution)/shard_map/all_gather | solution.py:132
  370.9 11.1 %gather_fusion.1 = bf16[2048,512]{1,0:T(8,128)(2,1)} fusion(bf16[2048,512]{1,0:T(8,128)(2,1)} %all-gather.7.cloned.1.call-done, s32[2048]{0:T(1024)S(1)} %broadcast_clamp_fusion), kind=kCustom, calls=%fused_computation.1 | custom fusion | bytes 4202496 | tf_op jit(solution)/shard_map/jit(_take)/gather | solution.py:144
  382.0 8.5 %convolution_convert_fusion = bf16[2048,2048]{1,0:T(8,128)(2,1)} fusion(bf16[1,512,2048]{2,1,0:T(8,128)(2,1)S(1)} %copy-done, bf16[2048,512]{1,0:T(8,128)(2,1)} %gather_fusion.1, pred[2048]{0:T(1024)(128)(4,1)S(1)} %get-tuple-element.69), kind=kOutput, calls=%fused_computation.40 | convolution fusion | flops 4300210176 | bytes 12584960 | tf_op jit(solution)/shard_map/dot_general | solution.py:147
  390.5 102.8 %reduce-scatter.5.cloned.1.call-done = bf16[128,2048]{1,0:T(8,128)(2,1)} async-done(((bf16[2048,2048]{1,0:T(8,128)(2,1)}), bf16[128,2048]{1,0:T(8,128)(2,1)}) %reduce-scatter.5.cloned.1.call-update) | async-done | bytes 524304 | tf_op jit(solution)/shard_map/reduce_scatter | solution.py:146
  493.3 10.5 %all_to_all.5 = bf16[2,64,2048]{2,1,0:T(8,128)(2,1)S(1)} all-to-all(bf16[2,64,2048]{2,1,0:T(8,128)(2,1)} %bitcast.117), channel_id=1, replica_groups=mesh['section'=2,'cp'=16,'tp'=4] {'section'}, dimensions={0} | all-to-all | bytes 1048576 | tf_op jit(solution)/shard_map/all_to_all | solution.py:153
  (121 shorter events, 50.2 us)
Async XLA Ops:
  6.5 375.4 %copy-start = (bf16[1,512,2048]{2,1,0:T(8,128)(2,1)S(1)}, bf16[1,512,2048]{2,1,0:T(8,128)(2,1)}, u32[]{:S(2)}) copy-start(bf16[1,512,2048]{2,1,0:T(8,128)(2,1)} %param.15) | copy-start | bytes 6291460
  6.5 71.5 %all-gather.5.cloned.1.call-start = ((), (), s32[]{:S(2)}) async-start(), calls=%async_computation.3 | async-start | bytes 8650752 | tf_op jit(solution)/shard_map/all_gather | solution.py:51
  7.3 239.9 %reduce-scatter.3.cloned.1.call-start = ((), (), s32[]{:S(2)}) async-start(), calls=%async_computation.4 | async-start | bytes 15728640 | tf_op jit(solution)/shard_map/reduce_scatter | solution.py:77
  98.8 16.5 %copy-start.5 = (f32[1,2048]{1,0:T(1,128)S(1)}, f32[1,2048]{1,0:T(1,128)}, u32[]{:S(2)}) copy-start(f32[1,2048]{1,0:T(1,128)} %param.13) | copy-start | bytes 24580
  135.4 116.5 %copy-start.6 = (s32[2]{0:T(128)S(1)}, s32[2]{0:T(128)}, u32[]{:S(2)}) copy-start(s32[2]{0:T(128)} %param.11) | copy-start | bytes 28
  135.4 173.6 %all-gather.9.cloned.1.call-start = ((), (), s32[]{:S(2)}) async-start(), calls=%async_computation.7 | async-start | bytes 2621440 | tf_op jit(solution)/shard_map/all_gather | solution.py:84
  249.3 1.1 copy-start.1
  251.5 119.4 %all-gather.7.cloned.1.call-start = ((), (), s32[]{:S(2)}) async-start(), calls=%async_computation.5 | async-start | bytes 2621440 | tf_op jit(solution)/shard_map/all_gather | solution.py:132
  251.5 18.1 %collective-permute-start = (bf16[512,512]{1,0:T(8,128)(2,1)}, bf16[512,512]{1,0:T(8,128)(2,1)}, u32[]{:S(2)}, u32[]{:S(2)}) collective-permute-start(bf16[512,512]{1,0:T(8,128)(2,1)} %get-tuple-element.81), channel_id=1, source_target_pairs={{0,1},{1,2},{2,3},{3,0},{4,5},{5,6},{6,7},{7,4},{8,9},{9,10},{10,1... | collective-permute-start | bytes 1572872 | tf_op jit(solution)/shard_map/ppermute | solution.py:17
  269.6 25.3 %collective-permute-start.1 = (bf16[512,512]{1,0:T(8,128)(2,1)}, bf16[512,512]{1,0:T(8,128)(2,1)}, u32[]{:S(2)}, u32[]{:S(2)}) collective-permute-start(bf16[512,512]{1,0:T(8,128)(2,1)} %collective-permute-done), channel_id=1, source_target_pairs={{0,1},{1,2},{2,3},{3,0},{4,5},{5,6},{6,7},{7,4},{8,9},{9,10},{10,1... | collective-permute-start | bytes 1572872 | tf_op jit(solution)/shard_map/ppermute | solution.py:17
  269.6 28.6 %collective-permute-start.2 = (bf16[512,512]{1,0:T(8,128)(2,1)}, bf16[512,512]{1,0:T(8,128)(2,1)}, u32[]{:S(2)}, u32[]{:S(2)}) collective-permute-start(bf16[512,512]{1,0:T(8,128)(2,1)} %get-tuple-element.81), channel_id=1, source_target_pairs={{0,3},{1,0},{2,1},{3,2},{4,7},{5,4},{6,5},{7,6},{8,11},{9,8},{10,9... | collective-permute-start | bytes 1572872 | tf_op jit(solution)/shard_map/ppermute | solution.py:19
  315.6 4.8 copy-start.2
  325.9 17.8 %copy-start.4 = (s32[32]{0:T(128)S(1)}, s32[32]{0:T(128)}, u32[]{:S(2)}) copy-start(s32[32]{0:T(128)} %param.12) | copy-start | bytes 388
  328.8 4.8 copy-start.3
  341.1 152.2 %reduce-scatter.5.cloned.1.call-start = ((), (), s32[]{:S(2)}) async-start(), calls=%async_computation.6 | async-start | bytes 8912896 | tf_op jit(solution)/shard_map/reduce_scatter | solution.py:146
Sparse Core Ops, SparseCore 0:
  9.1 68.9 all-gather.4
  135.5 111.6 reduce-scatter.2
  251.6 43.1 all-gather.8
  341.2 29.6 all-gather.6
  390.6 102.6 reduce-scatter.4
